TPU v7x, 256 devices: a whole 4x4x8 slice. The times are simulated.
256 devices in a mesh: req: 64 (over x, y_lo, z), tp: 4 (over y_hi, core).
Axes of the slice: x: 4, y: 4 (y_hi: 2, y_lo: 2; y = y_hi * 2 + y_lo), z: 8, core: 2. Of those that a mesh axis runs over, the one named last changes fastest.
Arguments:
- hidden_in: bfloat16 [8192, 2048], P('req')
- attn_gain: float32 [2048], replicated, may hold values from 0.1 to 1.9
- w_query: bfloat16 [2048, 2048], P(None, 'tp'), may hold values from -0.125 to 0.125
- w_keyval: bfloat16 [2048, 4, 256], P(None, 'tp'), may hold values from -0.125 to 0.125
- w_out: bfloat16 [2048, 2048], P('tp'), may hold values from -0.125 to 0.125
- moe_gain: float32 [2048], replicated, may hold values from 0.1 to 1.9
- w_gate_up: bfloat16 [64, 2, 2048, 1408], P('req', None, None, 'tp'), may hold values from -0.125 to 0.125
- w_down: bfloat16 [64, 1408, 2048], P('req', 'tp'), may hold values from -0.15625 to 0.15625
- seg_ids: int32 [64, 128], P('req'), may hold values from 0 to 3, never falling along the last dimension, each value on 1 to 64 neighbouring positions
- cached_len: int32 [64], P('req'), may hold values from 2048 to 4096, as said below
- page_table: int32 [64, 32], P('req'), may hold values from 0 to 1023, as said below
- cache_pool: bfloat16 [1024, 4, 128, 256], P('req', 'tp')
- expert_ids: int32 [8192, 6], P('req'), may hold values from 0 to 63, all different within a row; in each aligned block of 128 rows (0 to 127, 128 to 255, ...) at most 16 rows name the same one
- expert_weights: float32 [8192, 6], P('req'), may hold values from 0.05 to 0.5
Outputs:
- layer_out: bfloat16 [8192, 2048], P('req')
Inputs may be any that keep to these rules, and one draw needn't show every extreme that they name: `seg_ids`: row r holds the prompt numbers of pack r, never falling along the row; each prompt has 1 to 64 tokens, one exactly that many. `cached_len`: some pack has exactly 4096 cached tokens. `page_table`: entry j of row r names the page holding tokens j * 128 to (j + 1) * 128 - 1 of pack r's cached prefix; page p lies on index p // 16 of req. At most 1 entries of one row lie on one owner, and in every row some owner holds exactly 1. Entries past the cached length name pages too. `expert_ids`: each row names 6 different experts. Among the rows of one pack no expert is named more than 16 times, a bound that some block reaches.
All inputs are finite; a program needn't handle non-finite values.
Results may differ from a plain program's by a relative error of at most 0.009.
Values may be sent and summed in bfloat16 or wider, within the bound.
No kernel may reach another device: no remote copies, remote signals or barrier semaphores. Data moves between devices by JAX's collectives and lax.ppermute only.
A program may use at most 128 MiB of HBM per device.

v0:
```python
import math
import jax
import jax.numpy as jnp
from jax import lax
from jax.sharding import PartitionSpec as P

eps = 1e-06
rope_base = 600000.0


def rms_scale(rows_in, gain):
    widened = rows_in.astype(jnp.float32)
    return widened * lax.rsqrt(jnp.mean(widened * widened, axis=-1, keepdims=True) + eps) * gain


def rotate(vectors, angles):
    half_dim = vectors.shape[-1] // 2
    first_half = vectors[..., :half_dim]
    second_half = vectors[..., half_dim:]
    cosine = jnp.cos(angles)[:, None, :]
    sine_vals = jnp.sin(angles)[:, None, :]
    return jnp.concatenate(
        [
            first_half * cosine - second_half * sine_vals,
            second_half * cosine + first_half * sine_vals,
        ],
        axis=-1,
    )


def positions(segment_row, cached):
    length = segment_row.shape[0]
    token_index = jnp.arange(length, dtype=jnp.int32)
    begins = jnp.concatenate([jnp.ones((1,), dtype=bool), segment_row[1:] != segment_row[:-1]])
    seg_start = lax.cummax(jnp.where(begins, token_index, 0), axis=0)
    carried = segment_row == segment_row[0]
    place = token_index - seg_start + jnp.where(carried, cached, 0)
    return (place, carried)


def make_angles(place, head_dim):
    inverse = rope_base ** (-(jnp.arange(head_dim // 2, dtype=jnp.float32) * 2.0 / head_dim))
    return place.astype(jnp.float32)[:, None] * inverse[None, :]


def admit(segment_row, carried, cached, prefix_len):
    length = segment_row.shape[0]
    token_index = jnp.arange(length, dtype=jnp.int32)
    prefix_ok = (jnp.arange(prefix_len, dtype=jnp.int32)[None, :] < cached) & carried[:, None]
    local_ok = (segment_row[:, None] == segment_row[None, :]) & (
        token_index[None, :] <= token_index[:, None]
    )
    return jnp.concatenate([prefix_ok, local_ok], axis=1)


def attend(queries, all_keys, all_values, admitted):
    scale = 1.0 / math.sqrt(queries.shape[-1])
    scores = (
        jnp.einsum("tkgd,knd->kgtn", queries, all_keys, preferred_element_type=jnp.float32) * scale
    )
    scores = jnp.where(admitted[None, None], scores, -1e30)
    highest = jnp.max(scores, axis=-1, keepdims=True)
    expo = jnp.exp(scores - highest)
    totals = jnp.sum(expo, axis=-1, keepdims=True)
    weights = (expo / totals).astype(jnp.bfloat16)
    context = jnp.einsum("kgtn,knd->tkgd", weights, all_values, preferred_element_type=jnp.float32)
    return context.astype(jnp.bfloat16)


def shards(
    hidden_in,
    attn_gain,
    w_query,
    w_keyval,
    w_out,
    moe_gain,
    w_gate_up,
    w_down,
    seg_ids,
    cached_len,
    page_table,
    cache_pool,
    expert_ids,
    expert_weights,
):
    tok_rows, model_width = hidden_in.shape
    head_dim = w_keyval.shape[2] // 2
    kv_local = w_keyval.shape[1]
    q_local = w_query.shape[1] // head_dim
    group_size = q_local // kv_local
    segment_row = seg_ids[0]
    cached = cached_len[0]
    place, carried = positions(segment_row, cached)
    angles = make_angles(place, head_dim)
    normed = rms_scale(hidden_in, attn_gain).astype(jnp.bfloat16)
    n_req = lax.axis_size("req")
    listed = page_table[0]
    pref_pages = listed.shape[0]
    pages_dev = cache_pool.shape[0]
    page_len = cache_pool.shape[2]
    cap_pages = (2 * pref_pages + n_req - 1) // n_req
    owners = listed // pages_dev
    entry_index = jnp.arange(pref_pages, dtype=jnp.int32)
    earlier = (owners[None, :] == owners[:, None]) & (entry_index[None, :] < entry_index[:, None])
    owner_rank = jnp.sum(earlier.astype(jnp.int32), axis=1)
    page_slot = listed % pages_dev
    cap_index = jnp.arange(cap_pages, dtype=jnp.int32)
    owner_index = jnp.arange(n_req, dtype=jnp.int32)
    wanted = (owners[None, None, :] == owner_index[:, None, None]) & (
        owner_rank[None, None, :] == cap_index[None, :, None]
    )
    request = jnp.sum(jnp.where(wanted, page_slot[None, None, :], 0), axis=2)
    asked_slots = lax.all_to_all(request, "req", split_axis=0, concat_axis=0, tiled=True)
    served = cache_pool[asked_slots.reshape(-1)].reshape(
        n_req, cap_pages, kv_local, page_len, 2 * head_dim
    )
    fetched = lax.all_to_all(served, "req", split_axis=0, concat_axis=0, tiled=True)
    fetched = fetched.reshape(n_req * cap_pages, kv_local, page_len, 2 * head_dim)[
        owners * cap_pages + owner_rank
    ]
    prefix = jnp.transpose(fetched, (1, 0, 2, 3)).reshape(
        kv_local, pref_pages * page_len, 2 * head_dim
    )
    queries = jnp.dot(normed, w_query, preferred_element_type=jnp.float32).reshape(
        tok_rows, q_local, head_dim
    )
    queries = (
        rotate(queries, angles)
        .astype(jnp.bfloat16)
        .reshape(tok_rows, kv_local, group_size, head_dim)
    )
    keyval = jnp.dot(
        normed,
        w_keyval.reshape(model_width, kv_local * 2 * head_dim),
        preferred_element_type=jnp.float32,
    ).reshape(tok_rows, kv_local, 2 * head_dim)
    keys_new = rotate(keyval[..., :head_dim], angles).astype(jnp.bfloat16)
    values_new = keyval[..., head_dim:].astype(jnp.bfloat16)
    all_keys = jnp.concatenate([prefix[..., :head_dim], jnp.transpose(keys_new, (1, 0, 2))], axis=1)
    all_values = jnp.concatenate(
        [prefix[..., head_dim:], jnp.transpose(values_new, (1, 0, 2))], axis=1
    )
    admitted = admit(segment_row, carried, cached, pref_pages * page_len)
    context = attend(queries, all_keys, all_values, admitted).reshape(tok_rows, q_local * head_dim)
    attention = lax.psum(jnp.dot(context, w_out, preferred_element_type=jnp.float32), "tp")
    resid = (hidden_in.astype(jnp.float32) + attention).astype(jnp.bfloat16)
    moe_in = rms_scale(resid, moe_gain).astype(jnp.bfloat16)
    topk = expert_ids.shape[1]
    n_exp = n_req * w_gate_up.shape[0]
    cap_e = 4 * tok_rows * topk // (3 * n_exp)
    flat_ids = expert_ids.reshape(-1)
    onehot = (flat_ids[:, None] == jnp.arange(n_exp, dtype=jnp.int32)[None, :]).astype(jnp.int32)
    slot_rank = jnp.sum((jnp.cumsum(onehot, axis=0) - 1) * onehot, axis=1)
    assign_slot = flat_ids * cap_e + slot_rank
    slot_match = assign_slot[None, :] == jnp.arange(n_exp * cap_e, dtype=jnp.int32)[:, None]
    selector = jnp.any(slot_match.reshape(n_exp * cap_e, tok_rows, topk), axis=2).astype(
        jnp.bfloat16
    )
    n_tp = lax.axis_size("tp")
    tp_me = lax.axis_index("tp")
    cap_q = cap_e // n_tp
    sel_q = lax.dynamic_slice_in_dim(
        selector.reshape(n_exp, cap_e, tok_rows), tp_me * cap_q, cap_q, axis=1
    )
    outgoing = (
        jnp.einsum("ecs,sd->ecd", sel_q, moe_in, preferred_element_type=jnp.float32)
        .astype(jnp.bfloat16)
        .reshape(n_exp, cap_q * model_width)
    )
    expert_q = lax.all_to_all(outgoing, "req", split_axis=0, concat_axis=0, tiled=True)
    expert_in = lax.all_gather(expert_q, "tp", axis=1, tiled=True)
    expert_rows = expert_in.reshape(-1, model_width)
    gate_part = jnp.dot(expert_rows, w_gate_up[0, 0], preferred_element_type=jnp.float32)
    up_part = jnp.dot(expert_rows, w_gate_up[0, 1], preferred_element_type=jnp.float32)
    hidden_act = (jax.nn.silu(gate_part) * up_part).astype(jnp.bfloat16)
    partial = (
        jnp.dot(hidden_act, w_down[0], preferred_element_type=jnp.float32)
        .astype(jnp.bfloat16)
        .reshape(n_req, cap_e * model_width)
    )
    expert_share = lax.psum_scatter(partial, "tp", scatter_dimension=1, tiled=True)
    results_q = lax.all_to_all(expert_share, "req", split_axis=0, concat_axis=0, tiled=True)
    results = lax.all_gather(results_q, "tp", axis=1, tiled=True)
    picked = results.reshape(-1, model_width)[assign_slot].reshape(tok_rows, topk, model_width)
    moe_out = jnp.sum(expert_weights[:, :, None] * picked.astype(jnp.float32), axis=1)
    return (resid.astype(jnp.float32) + moe_out).astype(jnp.bfloat16)


def solution(mesh):
    in_specs = (
        P("req", None),
        P(),
        P(None, "tp"),
        P(None, "tp", None),
        P("tp", None),
        P(),
        P("req", None, None, "tp"),
        P("req", "tp", None),
        P("req", None),
        P("req"),
        P("req", None),
        P("req", "tp", None, None),
        P("req", None),
        P("req", None),
    )
    out_specs = P("req", None)
    return jax.shard_map(shards, mesh=mesh, in_specs=in_specs, out_specs=out_specs, check_vma=False)
```

profile of v0, /device:TPU:1, one launch (start us, length us, event | category | flops | bytes accessed | tf_op | source)
XLA Modules:
  0.0 605.5 jit_solution(16908138329106039818)
XLA Ops:
  8.4 22.6 %all_to_all.42 = s32[64,1,1]{2,1,0:T(1,128)S(1)} all-to-all(s32[64,1,1]{2,1,0:T(1,128)S(1)} %copy.63), channel_id=1, replica_groups=mesh['req'=64,'tp'=4] {'req'}, dimensions={0} | all-to-all | bytes 512 | tf_op jit(solution)/shard_map/all_to_all | solution.py:113
  32.2 4.0 gather_fusion
  36.2 5.8 all-to-all-start.1
  50.6 82.7 %all-to-all-done.1 = bf16[64,1,1,128,256]{4,3,2,1,0:T(8,128)(2,1)} async-done(((bf16[64,1,1,128,256]{4,3,2,1,0:T(8,128)(2,1)}), bf16[64,1,1,128,256]{4,3,2,1,0:T(8,128)(2,1)}, u32[]{:S(2)}, u32[]{:S(2)}) %all-to-all-start.1) | async-done | bytes 4194336 | tf_op jit(solution)/shard_map/all_to_all | solution.py:117
  133.3 4.2 gather_fusion.1
  149.0 48.8 %all-reduce.2.cloned.1.call-done = f32[128,2048]{1,0:T(8,128)} async-done(((f32[128,2048]{1,0:T(8,128)}), f32[128,2048]{1,0:T(8,128)}) %all-reduce.2.cloned.1.call-update) | async-done | bytes 1048592 | tf_op jit(solution)/shard_map/psum | solution.py:145
  201.6 6.2 %all_to_all.37 = bf16[64,1,8192]{2,1,0:T(2,128)(2,1)S(1)} reshape(bf16[64,4,2048]{2,1,0:T(4,128)(2,1)} %copy.76) | data formatting | bytes 2097152 | tf_op jit(solution)/shard_map/all_to_all | solution.py:170
  208.3 8.1 %reduce.11 = bf16[64,8192]{1,0:T(8,128)(2,1)} reduce(bf16[64,1,8192]{2,1,0:T(2,128)(2,1)S(1)} %all_to_all.37, bf16[]{:T(256)} %broadcast.486), dimensions={1}, to_apply=%all_to_all.37.reduce_sub_computation | reduce | bytes 2097154 | tf_op jit(solution)/shard_map/all_to_all | solution.py:170
  218.3 36.8 %all_to_all.43 = bf16[64,2,4096]{2,1,0:T(2,128)(2,1)S(1)} all-to-all(bf16[64,2,4096]{2,1,0:T(2,128)(2,1)S(1)} %reshape.700), channel_id=1, replica_groups=mesh['req'=64,'tp'=4] {'req'}, dimensions={0} | all-to-all | bytes 2097152 | tf_op jit(solution)/shard_map/all_to_all | solution.py:170
  255.1 3.5 reshape.701
  258.9 63.4 %all-gather.5.cloned.1.call-done = bf16[64,1,32768]{2,1,0:T(2,128)(2,1)} async-done(((bf16[64,1,8192]{2,1,0:T(2,128)(2,1)}), bf16[64,1,32768]{2,1,0:T(2,128)(2,1)}) %all-gather.5.cloned.1.call-update) | async-done | bytes 4194320 | tf_op jit(solution)/shard_map/all_gather | solution.py:171
  322.3 26.1 %reduce.6 = bf16[64,32768]{1,0:T(8,128)(2,1)} reduce(bf16[64,1,32768]{2,1,0:T(2,128)(2,1)} %all-gather.5.cloned.1.call-done, bf16[]{:T(256)} %constant.92), dimensions={1}, to_apply=%all-gather.reduce_sub_computation | reduce | bytes 8388610 | tf_op jit(solution)/shard_map/all_gather | solution.py:171
  348.4 7.4 %reshape.652 = bf16[1024,2048]{1,0:T(8,128)(2,1)} reshape(bf16[64,32768]{1,0:T(8,128)(2,1)} %reduce.6) | data formatting | bytes 8388608 | tf_op jit(solution)/shard_map/reshape | solution.py:172
  355.8 5.6 fusion.6
  361.4 9.0 %convolution_convert_fusion = bf16[1024,2048]{1,0:T(8,128)(2,1)} fusion(bf16[1,352,2048]{2,1,0:T(8,128)(2,1)S(1)} %copy-done.8, bf16[1024,2048]{1,0:T(8,128)(2,1)} %reshape.652, bf16[1,2,2048,352]{2,3,1,0:T(8,128)(2,1)} %param.20, f32[1024,352]{0,1:T(8,128)} %fusion.6), kind=kOutput, calls=%fused_computation.10 | convolution fusion | flops 2957049856 | bytes 12713984 | tf_op jit(solution)/shard_map/dot_general | solution.py:177
  370.4 7.4 %reshape.653 = bf16[64,32768]{1,0:T(8,128)(2,1)} reshape(bf16[1024,2048]{1,0:T(8,128)(2,1)} %convolution_convert_fusion) | data formatting | bytes 8388608 | tf_op jit(solution)/shard_map/reshape | solution.py:179
  377.9 55.6 %reduce-scatter.2.cloned.1.call-done = bf16[64,8192]{1,0:T(8,128)(2,1)} async-done(((bf16[64,32768]{1,0:T(8,128)(2,1)}), bf16[64,8192]{1,0:T(8,128)(2,1)}) %reduce-scatter.2.cloned.1.call-update) | async-done | bytes 1048592 | tf_op jit(solution)/shard_map/reduce_scatter | solution.py:181
  436.9 36.9 %all_to_all.44 = bf16[64,2,4096]{2,1,0:T(2,128)(2,1)S(1)} all-to-all(bf16[64,2,4096]{2,1,0:T(2,128)(2,1)S(1)} %reshape.702), channel_id=1, replica_groups=mesh['req'=64,'tp'=4] {'req'}, dimensions={0} | all-to-all | bytes 2097152 | tf_op jit(solution)/shard_map/all_to_all | solution.py:182
  477.7 63.5 %all-gather.7.cloned.1.call-done = bf16[64,1,32768]{2,1,0:T(2,128)(2,1)} async-done(((bf16[64,1,8192]{2,1,0:T(2,128)(2,1)}), bf16[64,1,32768]{2,1,0:T(2,128)(2,1)}) %all-gather.7.cloned.1.call-update) | async-done | bytes 4194320 | tf_op jit(solution)/shard_map/all_gather | solution.py:183
  541.2 26.1 %reduce.7 = bf16[64,32768]{1,0:T(8,128)(2,1)} reduce(bf16[64,1,32768]{2,1,0:T(2,128)(2,1)} %all-gather.7.cloned.1.call-done, bf16[]{:T(256)} %constant.92), dimensions={1}, to_apply=%all-gather.1.reduce_sub_computation | reduce | bytes 8388610 | tf_op jit(solution)/shard_map/all_gather | solution.py:183
  567.3 7.4 %reshape.654 = bf16[1024,2048]{1,0:T(8,128)(2,1)} reshape(bf16[64,32768]{1,0:T(8,128)(2,1)} %reduce.7) | data formatting | bytes 8388608 | tf_op jit(solution)/shard_map/reshape | solution.py:184
  574.7 9.8 %gather_fusion.2 = bf16[768,2048]{1,0:T(8,128)(2,1)} fusion(bf16[1024,2048]{1,0:T(8,128)(2,1)} %reshape.654, s32[1024]{0:T(1024)S(1)} %pad_clamp_fusion), kind=kCustom, calls=%fused_computation.2 | custom fusion | bytes 6294528 | tf_op jit(solution)/shard_map/gather | solution.py:184
  584.5 6.6 %reshape.655 = f32[128,6,2048]{2,1,0:T(8,128)} reshape(bf16[768,2048]{1,0:T(8,128)(2,1)} %gather_fusion.2) | data formatting | bytes 9437184 | tf_op jit(solution)/shard_map/convert_element_type | solution.py:185
  591.0 6.8 %multiply_reduce_fusion = f32[128,2048]{1,0:T(8,128)S(1)} fusion(f32[128,6,2048]{2,1,0:T(8,128)} %reshape.655, f32[128,6]{1,0:T(8,128)S(1)} %copy.69), kind=kLoop, calls=%fused_computation.6 | loop fusion | flops 2883584 | bytes 7343104 | tf_op jit(solution)/shard_map/reduce_sum | solution.py:185
  (92 shorter events, 36.9 us)
Async XLA Ops:
  6.5 136.9 %copy-start = (bf16[512,2048]{1,0:T(8,128)(2,1)S(1)}, bf16[512,2048]{1,0:T(8,128)(2,1)}, u32[]{:S(2)}) copy-start(bf16[512,2048]{1,0:T(8,128)(2,1)} %param.18) | copy-start | bytes 6291460
  36.2 6.5 %copy-start.5 = (s32[1,128]{1,0:T(1,128)S(1)}, s32[1,128]{1,0:T(1,128)}, u32[]{:S(2)}) copy-start(s32[1,128]{1,0:T(1,128)} %param.22) | copy-start | bytes 1540
  36.2 7.1 %copy-start.2 = (bf16[128,2048]{1,0:T(8,128)(2,1)S(1)}, bf16[128,2048]{1,0:T(8,128)(2,1)}, u32[]{:S(2)}) copy-start(bf16[128,2048]{1,0:T(8,128)(2,1)} %param.14) | copy-start | bytes 1572868
  36.2 7.3 %copy-start.3 = (f32[2048]{0:T(1024)S(1)}, f32[2048]{0:T(1024)}, u32[]{:S(2)}) copy-start(f32[2048]{0:T(1024)} %param.15) | copy-start | bytes 24580
  36.2 97.1 %all-to-all-start.1 = ((bf16[64,1,1,128,256]{4,3,2,1,0:T(8,128)(2,1)}), bf16[64,1,1,128,256]{4,3,2,1,0:T(8,128)(2,1)}, u32[]{:S(2)}, u32[]{:S(2)}) async-start(bf16[64,1,1,128,256]{4,3,2,1,0:T(8,128)(2,1)} %bitcast.127), calls=%async_computation.1 | async-start | bytes 8388608 | tf_op jit(solution)/shard_map/all_to_all | solution.py:117
  42.0 3.7 copy-start.9
  42.0 155.8 %all-reduce.2.cloned.1.call-start = ((), (), s32[]{:S(2)}) async-start(), calls=%async_computation.5 | async-start | bytes 2097152 | tf_op jit(solution)/shard_map/psum | solution.py:145
  143.4 2.1 copy-start.6
  144.9 54.3 %copy-start.4 = (f32[2048]{0:T(1024)S(1)}, f32[2048]{0:T(1024)}, u32[]{:S(2)}) copy-start(f32[2048]{0:T(1024)} %param.19) | copy-start | bytes 24580
  145.0 177.3 %all-gather.5.cloned.1.call-start = ((), (), s32[]{:S(2)}) async-start(), calls=%async_computation.7 | async-start | bytes 10485760 | tf_op jit(solution)/shard_map/all_gather | solution.py:171
  258.7 174.8 %reduce-scatter.2.cloned.1.call-start = ((), (), s32[]{:S(2)}) async-start(), calls=%async_computation.6 | async-start | bytes 5242880 | tf_op jit(solution)/shard_map/reduce_scatter | solution.py:181
  355.8 5.6 copy-start.8
  377.8 163.3 %all-gather.7.cloned.1.call-start = ((), (), s32[]{:S(2)}) async-start(), calls=%async_computation.8 | async-start | bytes 10485760 | tf_op jit(solution)/shard_map/all_gather | solution.py:183
  473.8 3.5 copy-start.7
  591.0 7.7 %copy-start.1 = (bf16[512,2048]{1,0:T(8,128)(2,1)S(1)}, bf16[512,2048]{1,0:T(8,128)(2,1)}, u32[]{:S(2)}) copy-start(bf16[512,2048]{1,0:T(8,128)(2,1)} %param.18) | copy-start | bytes 6291460
Sparse Core Ops, SparseCore 0:
  145.1 52.6 all-reduce.1
  258.8 63.4 all-gather.4
  377.9 55.4 reduce-scatter.1
  477.5 63.6 all-gather.6
where the time goes:
time: 615 us; the launch traced here: 605 us
  waiting for transfers between devices  314 us (51%)
  blocking collectives  96.3 us (16%)
  other arithmetic  82.4 us (13%)
  local copies, waits for them, and re-layouts  68.3 us (11%)
  matrix products  23.4 us (4%)
  between operations  14.4 us (2%)
  starting transfers between devices  6.6 us (1%)
    all_to_all x1, waiting for transfers between devices, shards(): lax.all_to_all(served, 'req', split_axis=0, concat_axis=0, tiled=True)  82.7 us
    all_gather x1, waiting for transfers between devices, shards(): results = lax.all_gather(results_q, 'tp', axis=1, tiled=True)  63.5 us
    all_gather x1, waiting for transfers between devices, shards(): expert_in = lax.all_gather(expert_q, 'tp', axis=1, tiled=True)  63.4 us
    reduce_scatter x1, waiting for transfers between devices, shards(): lax.psum_scatter(partial, 'tp', scatter_dimension=1, tiled=True)  55.6 us
    psum x1, waiting for transfers between devices, shards(): lax.psum(jnp.dot(context, w_out, preferred_element_type=jnp.float32), 'tp')  48.8 us
    all_to_all x1, blocking collectives, shards(): lax.all_to_all(expert_share, 'req', split_axis=0, concat_axis=0, tiled=True)  36.9 us
    all_to_all x1, blocking collectives, shards(): lax.all_to_all(outgoing, 'req', split_axis=0, concat_axis=0, tiled=True)  36.8 us
    all_gather x1, other arithmetic, shards(): results = lax.all_gather(results_q, 'tp', axis=1, tiled=True)  26.1 us
  transfers between devices with their start and end apart: 5, of which 5 were waited for; matrix products, arithmetic and copies ran while one was open for 2% of the time, Pallas kernels for 0%

commit v1 on v0

--- a/solution.py
+++ b/solution.py
@@ -6,6 +6,9 @@
 
 eps = 1e-06
 rope_base = 600000.0
+patch_cover = lambda x_local, join_dim: jnp.concatenate(
+    jax.lax.all_to_all(jnp.stack([x_local] * jax.lax.axis_size("tp"), 0), "tp", 0, 0), join_dim
+)
 
 
 def rms_scale(rows_in, gain):
@@ -180,7 +183,7 @@
     )
     expert_share = lax.psum_scatter(partial, "tp", scatter_dimension=1, tiled=True)
     results_q = lax.all_to_all(expert_share, "req", split_axis=0, concat_axis=0, tiled=True)
-    results = lax.all_gather(results_q, "tp", axis=1, tiled=True)
+    results = patch_cover(results_q, 1)
     picked = results.reshape(-1, model_width)[assign_slot].reshape(tok_rows, topk, model_width)
     moe_out = jnp.sum(expert_weights[:, :, None] * picked.astype(jnp.float32), axis=1)
     return (resid.astype(jnp.float32) + moe_out).astype(jnp.bfloat16)

time: 615 us -> 596 us (0.969)
  other arithmetic: 82.4 us -> 56.4 us
  waiting for transfers between devices: 314 us -> 299 us
  local copies, waits for them, and re-layouts: 68.3 us -> 82.5 us
  starting transfers between devices: 6.6 us -> 14.9 us
    all_gather x1 -> x0, waiting for transfers between devices: 63.5 us -> none  [shards(): results = lax.all_gather(results_q, 'tp', axis=1, tiled=True)]
    all_to_all x0 -> x1, waiting for transfers between devices: none -> 48.5 us  [jax.lax.all_to_all(jnp.stack([x_local] * jax.lax.axis_size('tp'), 0), 'tp...]
    all_gather x1 -> x0, other arithmetic: 26.1 us -> none  [shards(): results = lax.all_gather(results_q, 'tp', axis=1, tiled=True)]
    another operation x0 -> x2, local copies, waits for them, and re-layouts: none -> 10 us  [the longest x1 7.59 us: shards(): results.reshape(-1, model_width)[assign_slot]]
    all_to_all x0 -> x1, starting transfers between devices: none -> 8.31 us  [jax.lax.all_to_all(jnp.stack([x_local] * jax.lax.axis_size('tp'), 0), 'tp...]
    unnamed x26 -> x27, local copies, waits for them, and re-layouts: 9.89 us -> 14 us
where the time goes in v1:
time: 596 us; the launch traced here: 587 us
  waiting for transfers between devices  299 us (50%)
  blocking collectives  96.4 us (16%)
  local copies, waits for them, and re-layouts  82.5 us (14%)
  other arithmetic  56.4 us (9%)
  matrix products  23.4 us (4%)
  starting transfers between devices  14.9 us (2%)
  between operations  14.4 us (2%)
    all_to_all x1, waiting for transfers between devices, shards(): lax.all_to_all(served, 'req', split_axis=0, concat_axis=0, tiled=True)  82.7 us
    all_gather x1, waiting for transfers between devices, shards(): expert_in = lax.all_gather(expert_q, 'tp', axis=1, tiled=True)  63.4 us
    reduce_scatter x1, waiting for transfers between devices, shards(): lax.psum_scatter(partial, 'tp', scatter_dimension=1, tiled=True)  55.6 us
    psum x1, waiting for transfers between devices, shards(): lax.psum(jnp.dot(context, w_out, preferred_element_type=jnp.float32), 'tp')  48.8 us
    all_to_all x1, waiting for transfers between devices, jax.lax.all_to_all(jnp.stack([x_local] * jax.lax.axis_size('tp'), 0), 'tp...  48.5 us
    all_to_all x1, blocking collectives, shards(): lax.all_to_all(expert_share, 'req', split_axis=0, concat_axis=0, tiled=True)  37 us
    all_to_all x1, blocking collectives, shards(): lax.all_to_all(outgoing, 'req', split_axis=0, concat_axis=0, tiled=True)  36.8 us
    all_gather x1, other arithmetic, shards(): expert_in = lax.all_gather(expert_q, 'tp', axis=1, tiled=True)  26.1 us
  transfers between devices with their start and end apart: 5, of which 5 were waited for; matrix products, arithmetic and copies ran while one was open for 2% of the time, Pallas kernels for 0%

profile of v1, /device:TPU:1, one launch (start us, length us, event | category | flops | bytes accessed | tf_op | source)
XLA Modules:
  0.0 586.9 jit_solution(15287893992253916414)
XLA Ops:
  8.4 22.6 %all_to_all.44 = s32[64,1,1]{2,1,0:T(1,128)S(1)} all-to-all(s32[64,1,1]{2,1,0:T(1,128)S(1)} %copy.65), channel_id=1, replica_groups=mesh['req'=64,'tp'=4] {'req'}, dimensions={0} | all-to-all | bytes 512 | tf_op jit(solution)/shard_map/all_to_all | solution.py:116
  36.2 5.8 all-to-all-start.1
  50.6 82.7 %all-to-all-done.1 = bf16[64,1,1,128,256]{4,3,2,1,0:T(8,128)(2,1)} async-done(((bf16[64,1,1,128,256]{4,3,2,1,0:T(8,128)(2,1)}), bf16[64,1,1,128,256]{4,3,2,1,0:T(8,128)(2,1)}, u32[]{:S(2)}, u32[]{:S(2)}) %all-to-all-start.1) | async-done | bytes 4194336 | tf_op jit(solution)/shard_map/all_to_all | solution.py:120
  133.3 4.2 gather_fusion.1
  149.0 48.8 %all-reduce.2.cloned.1.call-done = f32[128,2048]{1,0:T(8,128)} async-done(((f32[128,2048]{1,0:T(8,128)}), f32[128,2048]{1,0:T(8,128)}) %all-reduce.2.cloned.1.call-update) | async-done | bytes 1048592 | tf_op jit(solution)/shard_map/psum | solution.py:148
  201.6 6.2 %all_to_all.38 = bf16[64,1,8192]{2,1,0:T(2,128)(2,1)S(1)} reshape(bf16[64,4,2048]{2,1,0:T(4,128)(2,1)} %copy.78) | data formatting | bytes 2097152 | tf_op jit(solution)/shard_map/all_to_all | solution.py:173
  208.3 8.1 %reduce.10 = bf16[64,8192]{1,0:T(8,128)(2,1)} reduce(bf16[64,1,8192]{2,1,0:T(2,128)(2,1)S(1)} %all_to_all.38, bf16[]{:T(256)} %broadcast.486), dimensions={1}, to_apply=%all_to_all.38.reduce_sub_computation | reduce | bytes 2097154 | tf_op jit(solution)/shard_map/all_to_all | solution.py:173
  218.3 36.8 %all_to_all.45 = bf16[64,2,4096]{2,1,0:T(2,128)(2,1)S(1)} all-to-all(bf16[64,2,4096]{2,1,0:T(2,128)(2,1)S(1)} %reshape.700), channel_id=1, replica_groups=mesh['req'=64,'tp'=4] {'req'}, dimensions={0} | all-to-all | bytes 2097152 | tf_op jit(solution)/shard_map/all_to_all | solution.py:173
  258.9 63.4 %all-gather.3.cloned.1.call-done = bf16[64,1,32768]{2,1,0:T(2,128)(2,1)} async-done(((bf16[64,1,8192]{2,1,0:T(2,128)(2,1)}), bf16[64,1,32768]{2,1,0:T(2,128)(2,1)}) %all-gather.3.cloned.1.call-update) | async-done | bytes 4194320 | tf_op jit(solution)/shard_map/all_gather | solution.py:174
  322.3 26.1 %reduce.6 = bf16[64,32768]{1,0:T(8,128)(2,1)} reduce(bf16[64,1,32768]{2,1,0:T(2,128)(2,1)} %all-gather.3.cloned.1.call-done, bf16[]{:T(256)} %constant.92), dimensions={1}, to_apply=%all-gather.reduce_sub_computation | reduce | bytes 8388610 | tf_op jit(solution)/shard_map/all_gather | solution.py:174
  348.4 7.4 %reshape.655 = bf16[1024,2048]{1,0:T(8,128)(2,1)} reshape(bf16[64,32768]{1,0:T(8,128)(2,1)} %reduce.6) | data formatting | bytes 8388608 | tf_op jit(solution)/shard_map/reshape | solution.py:175
  355.8 5.6 fusion.6
  361.4 9.0 %convolution_convert_fusion = bf16[1024,2048]{1,0:T(8,128)(2,1)} fusion(bf16[1,352,2048]{2,1,0:T(8,128)(2,1)S(1)} %copy-done.8, bf16[1024,2048]{1,0:T(8,128)(2,1)} %reshape.655, bf16[1,2,2048,352]{2,3,1,0:T(8,128)(2,1)} %param.20, f32[1024,352]{0,1:T(8,128)} %fusion.6), kind=kOutput, calls=%fused_computation.10 | convolution fusion | flops 2957049856 | bytes 12713984 | tf_op jit(solution)/shard_map/dot_general | solution.py:180
  370.4 7.4 %reshape.656 = bf16[64,32768]{1,0:T(8,128)(2,1)} reshape(bf16[1024,2048]{1,0:T(8,128)(2,1)} %convolution_convert_fusion) | data formatting | bytes 8388608 | tf_op jit(solution)/shard_map/reshape | solution.py:182
  377.8 55.6 %reduce-scatter.2.cloned.1.call-done = bf16[64,8192]{1,0:T(8,128)(2,1)} async-done(((bf16[64,32768]{1,0:T(8,128)(2,1)}), bf16[64,8192]{1,0:T(8,128)(2,1)}) %reduce-scatter.2.cloned.1.call-update) | async-done | bytes 1048592 | tf_op jit(solution)/shard_map/reduce_scatter | solution.py:184
  436.9 37.0 %all_to_all.46 = bf16[64,2,4096]{2,1,0:T(2,128)(2,1)} all-to-all(bf16[64,2,4096]{2,1,0:T(2,128)(2,1)S(1)} %reshape.702), channel_id=1, replica_groups=mesh['req'=64,'tp'=4] {'req'}, dimensions={0} | all-to-all | bytes 2097152 | tf_op jit(solution)/shard_map/all_to_all | solution.py:185
  473.9 6.5 %reshape.703 = bf16[64,1,8192]{2,1,0:T(2,128)(2,1)S(1)} reshape(bf16[64,2,4096]{2,1,0:T(2,128)(2,1)} %all_to_all.46) | data formatting | bytes 2097152
  484.0 8.3 %all-to-all-start.4 = ((bf16[4,64,8192]{2,1,0:T(8,128)(2,1)}), bf16[4,64,8192]{2,1,0:T(8,128)(2,1)}, u32[]{:S(2)}, u32[]{:S(2)}) async-start(bf16[4,64,8192]{2,1,0:T(8,128)(2,1)} %stack.10), calls=%async_computation.5 | async-start | bytes 8388608 | tf_op jit(solution)/shard_map/all_to_all | solution.py:10
  492.6 48.5 %all-to-all-done.4 = bf16[4,64,8192]{2,1,0:T(8,128)(2,1)} async-done(((bf16[4,64,8192]{2,1,0:T(8,128)(2,1)}), bf16[4,64,8192]{2,1,0:T(8,128)(2,1)}, u32[]{:S(2)}, u32[]{:S(2)}) %all-to-all-start.4) | async-done | bytes 4194336 | tf_op jit(solution)/shard_map/all_to_all | solution.py:10
  541.1 7.4 %copy.81 = bf16[64,4,8192]{2,1,0:T(4,128)(2,1)} copy(bf16[64,4,8192]{2,0,1:T(8,128)(2,1)} %bitcast.37) | data formatting | bytes 8388608 | tf_op jit(solution)/shard_map/reshape | solution.py:9
  548.5 7.6 %reshape_reshape.3 = bf16[1024,2048]{1,0:T(8,128)(2,1)} reshape(bf16[64,4,8192]{2,1,0:T(4,128)(2,1)} %copy.81) | data formatting | bytes 8388608 | tf_op jit(solution)/shard_map/reshape;reshape | solution.py:187
  556.1 9.8 %gather_fusion.2 = bf16[768,2048]{1,0:T(8,128)(2,1)} fusion(bf16[1024,2048]{1,0:T(8,128)(2,1)} %reshape_reshape.3, s32[1024]{0:T(1024)S(1)} %pad_clamp_fusion), kind=kCustom, calls=%fused_computation.2 | custom fusion | bytes 6294528 | tf_op jit(solution)/shard_map/gather | solution.py:187
  565.9 6.6 %reshape.658 = f32[128,6,2048]{2,1,0:T(8,128)} reshape(bf16[768,2048]{1,0:T(8,128)(2,1)} %gather_fusion.2) | data formatting | bytes 9437184 | tf_op jit(solution)/shard_map/convert_element_type | solution.py:188
  572.5 6.8 %multiply_reduce_fusion = f32[128,2048]{1,0:T(8,128)S(1)} fusion(f32[128,6,2048]{2,1,0:T(8,128)} %reshape.658, f32[128,6]{1,0:T(8,128)S(1)} %copy.71), kind=kLoop, calls=%fused_computation.6 | loop fusion | flops 2883584 | bytes 7343104 | tf_op jit(solution)/shard_map/reduce_sum | solution.py:188
  (93 shorter events, 44.4 us)
Async XLA Ops:
  6.5 136.9 %copy-start = (bf16[512,2048]{1,0:T(8,128)(2,1)S(1)}, bf16[512,2048]{1,0:T(8,128)(2,1)}, u32[]{:S(2)}) copy-start(bf16[512,2048]{1,0:T(8,128)(2,1)} %param.18) | copy-start | bytes 6291460
  36.2 6.5 %copy-start.5 = (s32[1,128]{1,0:T(1,128)S(1)}, s32[1,128]{1,0:T(1,128)}, u32[]{:S(2)}) copy-start(s32[1,128]{1,0:T(1,128)} %param.22) | copy-start | bytes 1540
  36.2 7.1 %copy-start.2 = (bf16[128,2048]{1,0:T(8,128)(2,1)S(1)}, bf16[128,2048]{1,0:T(8,128)(2,1)}, u32[]{:S(2)}) copy-start(bf16[128,2048]{1,0:T(8,128)(2,1)} %param.14) | copy-start | bytes 1572868
  36.2 7.3 %copy-start.3 = (f32[2048]{0:T(1024)S(1)}, f32[2048]{0:T(1024)}, u32[]{:S(2)}) copy-start(f32[2048]{0:T(1024)} %param.15) | copy-start | bytes 24580
  36.2 97.1 %all-to-all-start.1 = ((bf16[64,1,1,128,256]{4,3,2,1,0:T(8,128)(2,1)}), bf16[64,1,1,128,256]{4,3,2,1,0:T(8,128)(2,1)}, u32[]{:S(2)}, u32[]{:S(2)}) async-start(bf16[64,1,1,128,256]{4,3,2,1,0:T(8,128)(2,1)} %bitcast.131), calls=%async_computation.1 | async-start | bytes 8388608 | tf_op jit(solution)/shard_map/all_to_all | solution.py:120
  42.0 3.7 copy-start.9
  42.0 155.8 %all-reduce.2.cloned.1.call-start = ((), (), s32[]{:S(2)}) async-start(), calls=%async_computation.6 | async-start | bytes 2097152 | tf_op jit(solution)/shard_map/psum | solution.py:148
  143.4 2.1 copy-start.6
  144.9 54.3 %copy-start.4 = (f32[2048]{0:T(1024)S(1)}, f32[2048]{0:T(1024)}, u32[]{:S(2)}) copy-start(f32[2048]{0:T(1024)} %param.19) | copy-start | bytes 24580
  145.0 177.3 %all-gather.3.cloned.1.call-start = ((), (), s32[]{:S(2)}) async-start(), calls=%async_computation.8 | async-start | bytes 10485760 | tf_op jit(solution)/shard_map/all_gather | solution.py:174
  258.7 174.8 %reduce-scatter.2.cloned.1.call-start = ((), (), s32[]{:S(2)}) async-start(), calls=%async_computation.7 | async-start | bytes 5242880 | tf_op jit(solution)/shard_map/reduce_scatter | solution.py:184
  355.8 5.6 copy-start.8
  484.0 8.3 %copy-start.7 = (f32[128,6]{0,1:T(8,128)S(1)}, f32[128,6]{0,1:T(8,128)}, u32[]{:S(2)}) copy-start(f32[128,6]{0,1:T(8,128)} %param.27) | copy-start | bytes 9220
  484.0 57.1 %all-to-all-start.4 = ((bf16[4,64,8192]{2,1,0:T(8,128)(2,1)}), bf16[4,64,8192]{2,1,0:T(8,128)(2,1)}, u32[]{:S(2)}, u32[]{:S(2)}) async-start(bf16[4,64,8192]{2,1,0:T(8,128)(2,1)} %stack.10), calls=%async_computation.5 | async-start | bytes 8388608 | tf_op jit(solution)/shard_map/all_to_all | solution.py:10
  572.5 7.7 %copy-start.1 = (bf16[512,2048]{1,0:T(8,128)(2,1)S(1)}, bf16[512,2048]{1,0:T(8,128)(2,1)}, u32[]{:S(2)}) copy-start(bf16[512,2048]{1,0:T(8,128)(2,1)} %param.18) | copy-start | bytes 6291460
Sparse Core Ops, SparseCore 0:
  145.1 52.6 all-reduce.1
  258.8 63.4 all-gather.2
  377.9 55.4 reduce-scatter.1
